TPU v7x, 128 devices: a whole 4x4x4 slice. The times are simulated.
128 devices in a mesh: row: 16 (over z_lo, x, core), col: 8 (over y, z_hi).
Axes of the slice: x: 4, y: 4, z: 4 (z_hi: 2, z_lo: 2; z = z_hi * 2 + z_lo), core: 2. Of those that a mesh axis runs over, the one named last changes fastest.
Arguments:
- slab_embed: float32 [65536, 768], P(('col', 'row')), may hold values from -1 to 1
- coverage_old: float32 [65536], P('col'), may hold values from 2 to 4.5
- sel_index: int32 [2048], P('row'), may hold values from 0 to 65535
- cand_index: int32 [3072], P('row'), may hold values from 0 to 65535
Outputs:
- coverage: float32 [65536], P('col')
- total_gain: float32 [3072], P('row')
Inputs may be any that keep to these rules, and one draw needn't show every extreme that they name: `sel_index`: indices into the slab. `cand_index`: indices into the slab.
All inputs are finite; a program needn't handle non-finite values.
Results may differ from a plain program's by a relative error of at most 0.00014.
Values sent between devices are 32-bit elements; how exact they have to be, the bound alone decides.
No kernel may reach another device: no remote copies, remote signals or barrier semaphores. Data moves between devices by JAX's collectives and lax.ppermute only.
A program may use at most 128 MiB of HBM per device.

v0:
```python
import jax
import jax.numpy as jnp
from jax import lax
from jax.sharding import Mesh
from jax.sharding import PartitionSpec as P

N_Y, N_Z = (4, 2)


def similar(left, right):
    return lax.dot_general(
        left,
        right,
        (((1,), (1,)), ((), ())),
        precision=lax.Precision.HIGH,
        preferred_element_type=jnp.float32,
    )


def lookup(source, indices, first_row):
    position = indices - first_row
    inside = (position >= 0) & (position < source.shape[0])
    picked = jnp.take(source, jnp.clip(position, 0, source.shape[0] - 1), axis=0)
    return jnp.where(inside[:, None], picked, 0.0)


def col_of(y, z):
    return y % N_Y * N_Z + z


def y_shift(value, step):
    pairs = [(col_of(y, z), col_of(y + step, z)) for y in range(N_Y) for z in range(N_Z)]
    return lax.ppermute(value, "col", pairs)


def pair_split(value, low):
    halves = value.reshape(2, value.shape[0] // 2, *value.shape[1:])
    return (jnp.where(low, halves[0], halves[1]), jnp.where(low, halves[1], halves[0]))


def pair_join(mine, other, low):
    return jnp.where(low, jnp.concatenate([mine, other]), jnp.concatenate([other, mine]))


def z_group_shift(value, k):
    if k == 1:
        return lax.ppermute(value, "col", [(c, c ^ 1) for c in range(N_Y * N_Z)])
    if k == 2:
        return lax.ppermute(value, "zl", [(0, 1), (1, 0)])
    n = 2 * N_Y * N_Z
    return lax.ppermute(value, ("zl", "col"), [(i, i ^ N_Y * N_Z ^ 1) for i in range(n)])


def group_masked_sum(value):
    here = lax.axis_index("col")
    y, z = (here // N_Z, here % N_Z)
    g = lax.axis_index("zl") * 2 + z
    quarter = value.shape[0] // N_Y

    def part(k):
        return lax.dynamic_slice_in_dim(value, (y + k) % N_Y * quarter, quarter)

    own = part(0)
    for k in range(1, N_Y):
        own = own + y_shift(part(k), k)
    piece = quarter // 4

    def z_part(k):
        return lax.dynamic_slice_in_dim(own, (g ^ k) * piece, piece)

    mine = z_part(0)
    for k in range(1, 4):
        mine = mine + z_group_shift(z_part(k), k)
    received = jnp.stack([mine] + [z_group_shift(mine, k) for k in range(1, 4)])
    own = jnp.take(received, jnp.arange(4) ^ g, axis=0).reshape(own.shape)
    pieces = [own] + [y_shift(own, -k) for k in range(1, N_Y)]
    return jnp.roll(jnp.stack(pieces), y, axis=0).reshape(value.shape)


def all_max_two_rounds(value, axis, n):
    for bits in ((1, 2, 3), (4,)):
        received = [lax.ppermute(value, axis, [(i, i ^ k) for i in range(n)]) for k in bits]
        for other in received:
            value = jnp.maximum(value, other)
    return value


def group_sum_in_order(value):
    here = lax.axis_index("col")
    y, z = (here // N_Z, here % N_Z)
    g = lax.axis_index("zl") * 2 + z
    received = jnp.stack([value] + [z_group_shift(value, k) for k in range(1, 4)])
    z_sum = jnp.sum(jnp.take(received, jnp.arange(4) ^ g, axis=0), axis=0)
    col_pairs = [[(c, c ^ 2 * k) for c in range(N_Y * N_Z)] for k in range(1, N_Y)]
    received = jnp.stack([z_sum] + [lax.ppermute(z_sum, "col", pairs) for pairs in col_pairs])
    return jnp.sum(jnp.take(received, jnp.arange(N_Y) ^ y, axis=0), axis=0)


def all_max(value, axis, n):
    bit = 1
    while bit < n:
        value = jnp.maximum(value, lax.ppermute(value, axis, [(i, i ^ bit) for i in range(n)]))
        bit *= 2
    return value


def gather_in_order(parts, axis, n):
    here = lax.axis_index(axis)
    bit = 1
    while bit < n:
        other = lax.ppermute(parts, axis, [(i, i ^ bit) for i in range(n)])
        low = here & bit == 0
        parts = jnp.where(low, jnp.concatenate([parts, other]), jnp.concatenate([other, parts]))
        bit *= 2
    return parts


def body(slab_embed, coverage_old, sel_index, cand_index):
    n_xc = 8
    col_id = lax.axis_index("col")
    zl = lax.axis_index("zl")
    half = lax.all_gather(slab_embed, "xc", axis=0, tiled=True)
    first_row = (col_id * 2 + zl) * half.shape[0]
    zl_swap = [(0, 1), (1, 0)]
    both_sel = pair_join(sel_index, lax.ppermute(sel_index, "zl", zl_swap), zl == 0)
    both_cand = pair_join(cand_index, lax.ppermute(cand_index, "zl", zl_swap), zl == 0)
    selected = group_masked_sum(lookup(half, both_sel, first_row))
    chosen = group_masked_sum(lookup(half, both_cand, first_row))
    n_sel = both_sel.shape[0]
    sel_scores = lax.optimization_barrier(similar(selected, half))
    reached = all_max_two_rounds(jnp.max(sel_scores, axis=0), "xc", n_xc)
    old = lax.dynamic_slice_in_dim(coverage_old, zl * half.shape[0], half.shape[0])
    coverage = jnp.maximum(old, reached)
    gain_part = jnp.sum(jnp.maximum(similar(chosen, half) - coverage[None, :], 0.0), axis=1)
    total = group_sum_in_order(gain_part)
    total_gain = lax.dynamic_slice_in_dim(total, zl * cand_index.shape[0], cand_index.shape[0])
    full_coverage = pair_join(coverage, lax.ppermute(coverage, "zl", zl_swap), zl == 0)
    return (full_coverage, total_gain)


def solution(mesh):
    shape = dict(zip(mesh.axis_names, mesh.devices.shape))
    names, sizes = ([], [])
    for name in mesh.axis_names:
        if name == "row":
            names += ["zl", "xc"]
            sizes += [2, shape["row"] // 2]
        else:
            names.append(name)
            sizes.append(shape[name])
    split = Mesh(mesh.devices.reshape(sizes), tuple(names))
    in_specs = (P(("col", "zl", "xc"), None), P("col"), P(("zl", "xc")), P(("zl", "xc")))
    out_specs = (P("col"), P(("zl", "xc")))
    return jax.shard_map(body, mesh=split, in_specs=in_specs, out_specs=out_specs, check_vma=False)
```

profile of v0, /device:TPU:8, one launch (start us, length us, event | category | flops | bytes accessed | tf_op | source)
XLA Modules:
  0.0 208.8 jit_solution(17445739290626050738)
XLA Ops:
  7.9 2.0 collective-permute-start
  14.2 65.1 %all-gather.2.cloned.1.call-done = f32[4096,768]{1,0:T(8,128)} async-done(((f32[512,768]{1,0:T(8,128)}), f32[4096,768]{1,0:T(8,128)}) %all-gather.2.cloned.1.call-update) | async-done | bytes 12582928 | tf_op jit(solution)/shard_map/all_gather | solution.py:122
  79.3 6.0 %gather_fusion = f32[256,768]{1,0:T(8,128)S(1)} fusion(f32[4096,768]{1,0:T(8,128)} %all-gather.2.cloned.1.call-done, s32[1024]{0:T(1024)S(1)} %pad_clamp_fusion.4), kind=kCustom, calls=%fused_computation.2 | custom fusion | bytes 1573888 | tf_op jit(solution)/shard_map/jit(_take)/gather | solution.py:23
  86.9 2.4 %collective-permute-start.2 = (f32[64,768]{1,0:T(8,128)}, f32[64,768]{1,0:T(8,128)}, u32[]{:S(2)}, u32[]{:S(2)}) collective-permute-start(f32[64,768]{1,0:T(8,128)} %get-tuple-element.10), channel_id=1, source_target_pairs={{0,4},{1,5},{2,6},{3,7},{4,0},{5,1},{6,2},{7,3},{8,12},{9,13},{10,... | collective-permute-start | bytes 589832 | tf_op jit(solution)/shard_map/ppermute | solution.py:33
  91.1 7.1 %gather_fusion.2 = f32[384,768]{1,0:T(8,128)S(1)} fusion(f32[4096,768]{1,0:T(8,128)} %all-gather.2.cloned.1.call-done, s32[1024]{0:T(1024)S(1)} %pad_clamp_fusion.2), kind=kCustom, calls=%fused_computation.4 | custom fusion | bytes 2360832 | tf_op jit(solution)/shard_map/jit(_take)/gather | solution.py:23
  100.8 3.0 %collective-permute-start.6 = (f32[16,768]{1,0:T(8,128)S(1)}, f32[16,768]{1,0:T(8,128)S(1)}, u32[]{:S(2)}, u32[]{:S(2)}) collective-permute-start(f32[16,768]{1,0:T(8,128)S(1)} %get-tuple-element.15), channel_id=1, source_target_pairs={{0,65},{1,64},{2,67},{3,66},{4,69},{5,68},{6,71},{7,70},{64,1},{65... | collective-permute-start | bytes 147464 | tf_op jit(solution)/shard_map/ppermute | solution.py:51
  103.9 2.7 %collective-permute-start.21 = (f32[96,768]{1,0:T(8,128)S(1)}, f32[96,768]{1,0:T(8,128)S(1)}, u32[]{:S(2)}, u32[]{:S(2)}) collective-permute-start(f32[96,768]{1,0:T(8,128)S(1)} %get-tuple-element.6), channel_id=1, source_target_pairs={{0,6},{1,7},{2,0},{3,1},{4,2},{5,3},{6,4},{7,5},{8,14},{9,15},{10,... | collective-permute-start | bytes 884744 | tf_op jit(solution)/shard_map/ppermute | solution.py:33
  110.8 2.0 collective-permute-done.5
  116.6 2.7 %collective-permute-start.7 = (f32[16,768]{1,0:T(8,128)S(1)}, f32[16,768]{1,0:T(8,128)S(1)}, u32[]{:S(2)}, u32[]{:S(2)}) collective-permute-start(f32[16,768]{1,0:T(8,128)S(1)} %add_add_fusion.3), channel_id=1, source_target_pairs={{0,1},{1,0},{2,3},{3,2},{4,5},{5,4},{6,7},{7,6},{8,9},{9,8},{10,11... | collective-permute-start | bytes 147464 | tf_op jit(solution)/shard_map/ppermute | solution.py:47
  121.4 4.1 %collective-permute-start.22 = (f32[24,768]{1,0:T(8,128)S(1)}, f32[24,768]{1,0:T(8,128)S(1)}, u32[]{:S(2)}, u32[]{:S(2)}) collective-permute-start(f32[24,768]{1,0:T(8,128)S(1)} %get-tuple-element.11), channel_id=1, source_target_pairs={{0,1},{1,0},{2,3},{3,2},{4,5},{5,4},{6,7},{7,6},{8,9},{9,8},{10,11... | collective-permute-start | bytes 221192 | tf_op jit(solution)/shard_map/ppermute | solution.py:47
  126.1 2.7 %collective-permute-start.10 = (f32[64,768]{1,0:T(8,128)S(1)}, f32[64,768]{1,0:T(8,128)S(1)}, u32[]{:S(2)}, u32[]{:S(2)}) collective-permute-start(f32[64,768]{1,0:T(8,128)S(1)} %bitcast_select_fusion.2), channel_id=1, source_target_pairs={{0,6},{1,7},{2,0},{3,1},{4,2},{5,3},{6,4},{7,5},{8,14},{9,15},{10,... | collective-permute-start | bytes 589832 | tf_op jit(solution)/shard_map/ppermute | solution.py:33
  131.4 2.5 %collective-permute-start.25 = (f32[24,768]{1,0:T(8,128)S(1)}, f32[24,768]{1,0:T(8,128)S(1)}, u32[]{:S(2)}, u32[]{:S(2)}) collective-permute-start(f32[24,768]{1,0:T(8,128)S(1)} %add_add_fusion.2), channel_id=1, source_target_pairs={{0,1},{1,0},{2,3},{3,2},{4,5},{5,4},{6,7},{7,6},{8,9},{9,8},{10,11... | collective-permute-start | bytes 221192 | tf_op jit(solution)/shard_map/ppermute | solution.py:47
  137.9 3.3 %collective-permute-done.12 = f32[64,768]{1,0:T(8,128)S(1)} collective-permute-done((f32[64,768]{1,0:T(8,128)S(1)}, f32[64,768]{1,0:T(8,128)S(1)}, u32[]{:S(2)}, u32[]{:S(2)}) %collective-permute-start.12) | collective-permute-done | bytes 196640 | tf_op jit(solution)/shard_map/ppermute | solution.py:33
  141.5 10.3 %fusion.13 = f32[256,4096]{1,0:T(8,128)} fusion(f32[256,768]{1,0:T(8,128)S(1)} %bitcast.61, f32[4096,768]{1,0:T(8,128)} %all-gather.2.cloned.1.call-done), kind=kOutput, calls=%fused_computation.86 | convolution fusion | flops 4831838208 | bytes 17563648 | tf_op jit(solution)/shard_map/dot_general | solution.py:11
  151.8 2.4 %reduce_max.9 = f32[4096]{0:T(1024)S(1)} reduce(f32[256,4096]{1,0:T(8,128)} %fusion.13, f32[]{:T(128)} %constant.182.clone.1), dimensions={0}, to_apply=%region_0.1 | reduce | flops 1044480 | bytes 4210692 | tf_op jit(solution)/shard_map/reduce_max | solution.py:131
  156.2 3.3 %collective-permute-start.28 = (f32[96,768]{1,0:T(8,128)S(1)}, f32[96,768]{1,0:T(8,128)S(1)}, u32[]{:S(2)}, u32[]{:S(2)}) collective-permute-start(f32[96,768]{1,0:T(8,128)S(1)} %bitcast_select_fusion), channel_id=1, source_target_pairs={{0,6},{1,7},{2,0},{3,1},{4,2},{5,3},{6,4},{7,5},{8,14},{9,15},{10,... | collective-permute-start | bytes 884744 | tf_op jit(solution)/shard_map/ppermute | solution.py:33
  159.5 2.3 %collective-permute-start.30 = (f32[96,768]{1,0:T(8,128)S(1)}, f32[96,768]{1,0:T(8,128)S(1)}, u32[]{:S(2)}, u32[]{:S(2)}) collective-permute-start(f32[96,768]{1,0:T(8,128)S(1)} %bitcast_select_fusion), channel_id=1, source_target_pairs={{0,2},{1,3},{2,4},{3,5},{4,6},{5,7},{6,0},{7,1},{8,10},{9,11},{10,... | collective-permute-start | bytes 884744 | tf_op jit(solution)/shard_map/ppermute | solution.py:33
  161.8 2.2 %collective-permute-start.16 = (f32[4096]{0:T(1024)S(1)}, f32[4096]{0:T(1024)S(1)}, u32[]{:S(2)}, u32[]{:S(2)}) collective-permute-start(f32[4096]{0:T(1024)S(1)} %maximum_maximum_fusion.1), channel_id=1, source_target_pairs={{0,32},{8,40},{16,48},{24,56},{32,0},{40,8},{48,16},{56,24},{1,33}... | collective-permute-start | bytes 49160 | tf_op jit(solution)/shard_map/ppermute | solution.py:82
  164.1 3.0 %collective-permute-done.16 = f32[4096]{0:T(1024)S(1)} collective-permute-done((f32[4096]{0:T(1024)S(1)}, f32[4096]{0:T(1024)S(1)}, u32[]{:S(2)}, u32[]{:S(2)}) %collective-permute-start.16) | collective-permute-done | bytes 16416 | tf_op jit(solution)/shard_map/ppermute | solution.py:82
  167.2 5.5 %collective-permute-done.29 = f32[96,768]{1,0:T(8,128)S(1)} collective-permute-done((f32[96,768]{1,0:T(8,128)S(1)}, f32[96,768]{1,0:T(8,128)S(1)}, u32[]{:S(2)}, u32[]{:S(2)}) %collective-permute-start.29) | collective-permute-done | bytes 294944 | tf_op jit(solution)/shard_map/ppermute | solution.py:33
  173.9 10.8 %maximum_reduce_fusion = f32[384]{0:T(512)S(1)} fusion(f32[384,768]{1,0:T(8,128)S(1)} %bitcast.64, f32[4096,768]{1,0:T(8,128)} %all-gather.2.cloned.1.call-done, f32[4096]{0:T(1024)S(1)} %maximum_maximum_fusion), kind=kOutput, calls=%fused_computation.6 | convolution fusion | flops 7252475392 | bytes 13780480 | tf_op jit(solution)/shard_map/dot_general | solution.py:11
  185.8 3.7 %collective-permute-start.31 = (f32[384]{0:T(512)S(1)}, f32[384]{0:T(512)S(1)}, u32[]{:S(2)}, u32[]{:S(2)}) collective-permute-start(f32[384]{0:T(512)S(1)} %maximum_reduce_fusion), channel_id=1, source_target_pairs={{0,1},{1,0},{2,3},{3,2},{4,5},{5,4},{6,7},{7,6},{8,9},{9,8},{10,11... | collective-permute-start | bytes 4616 | tf_op jit(solution)/shard_map/ppermute | solution.py:47
  193.2 3.9 %collective-permute-start.35 = (f32[384]{0:T(512)S(1)}, f32[384]{0:T(512)S(1)}, u32[]{:S(2)}, u32[]{:S(2)}) collective-permute-start(f32[384]{0:T(512)S(1)} %select_reduce_fusion.1), channel_id=1, source_target_pairs={{0,4},{1,5},{2,6},{3,7},{4,0},{5,1},{6,2},{7,3},{8,12},{9,13},{10,... | collective-permute-start | bytes 4616 | tf_op jit(solution)/shard_map/ppermute | solution.py:95
  198.7 2.0 collective-permute-done.34
  (134 shorter events, 39.2 us)
Async XLA Ops:
  7.2 72.2 %all-gather.2.cloned.1.call-start = ((), (), s32[]{:S(2)}) async-start(), calls=%async_computation | async-start | bytes 14155776 | tf_op jit(solution)/shard_map/all_gather | solution.py:122
  86.3 12.7 %collective-permute-start.3 = (f32[64,768]{1,0:T(8,128)}, f32[64,768]{1,0:T(8,128)S(1)}, u32[]{:S(2)}, u32[]{:S(2)}) collective-permute-start(f32[64,768]{1,0:T(8,128)} %get-tuple-element.9), channel_id=1, source_target_pairs={{0,6},{1,7},{2,0},{3,1},{4,2},{5,3},{6,4},{7,5},{8,14},{9,15},{10,... | collective-permute-start | bytes 589832 | tf_op jit(solution)/shard_map/ppermute | solution.py:33
  86.9 12.2 %collective-permute-start.2 = (f32[64,768]{1,0:T(8,128)}, f32[64,768]{1,0:T(8,128)}, u32[]{:S(2)}, u32[]{:S(2)}) collective-permute-start(f32[64,768]{1,0:T(8,128)} %get-tuple-element.10), channel_id=1, source_target_pairs={{0,4},{1,5},{2,6},{3,7},{4,0},{5,1},{6,2},{7,3},{8,12},{9,13},{10,... | collective-permute-start | bytes 589832 | tf_op jit(solution)/shard_map/ppermute | solution.py:33
  89.3 10.5 %collective-permute-start.1 = (f32[64,768]{1,0:T(8,128)S(1)}, f32[64,768]{1,0:T(8,128)}, u32[]{:S(2)}, u32[]{:S(2)}) collective-permute-start(f32[64,768]{1,0:T(8,128)S(1)} %get-tuple-element.8), channel_id=1, source_target_pairs={{0,2},{1,3},{2,4},{3,5},{4,6},{5,7},{6,0},{7,1},{8,10},{9,11},{10,... | collective-permute-start | bytes 589832 | tf_op jit(solution)/shard_map/ppermute | solution.py:33
  100.8 8.1 %collective-permute-start.6 = (f32[16,768]{1,0:T(8,128)S(1)}, f32[16,768]{1,0:T(8,128)S(1)}, u32[]{:S(2)}, u32[]{:S(2)}) collective-permute-start(f32[16,768]{1,0:T(8,128)S(1)} %get-tuple-element.15), channel_id=1, source_target_pairs={{0,65},{1,64},{2,67},{3,66},{4,69},{5,68},{6,71},{7,70},{64,1},{65... | collective-permute-start | bytes 147464 | tf_op jit(solution)/shard_map/ppermute | solution.py:51
  103.9 12.6 %collective-permute-start.21 = (f32[96,768]{1,0:T(8,128)S(1)}, f32[96,768]{1,0:T(8,128)S(1)}, u32[]{:S(2)}, u32[]{:S(2)}) collective-permute-start(f32[96,768]{1,0:T(8,128)S(1)} %get-tuple-element.6), channel_id=1, source_target_pairs={{0,6},{1,7},{2,0},{3,1},{4,2},{5,3},{6,4},{7,5},{8,14},{9,15},{10,... | collective-permute-start | bytes 884744 | tf_op jit(solution)/shard_map/ppermute | solution.py:33
  106.7 13.1 %collective-permute-start.20 = (f32[96,768]{1,0:T(8,128)S(1)}, f32[96,768]{1,0:T(8,128)S(1)}, u32[]{:S(2)}, u32[]{:S(2)}) collective-permute-start(f32[96,768]{1,0:T(8,128)S(1)} %get-tuple-element.7), channel_id=1, source_target_pairs={{0,4},{1,5},{2,6},{3,7},{4,0},{5,1},{6,2},{7,3},{8,12},{9,13},{10,... | collective-permute-start | bytes 884744 | tf_op jit(solution)/shard_map/ppermute | solution.py:33
  106.9 13.7 %collective-permute-start.19 = (f32[96,768]{1,0:T(8,128)S(1)}, f32[96,768]{1,0:T(8,128)S(1)}, u32[]{:S(2)}, u32[]{:S(2)}) collective-permute-start(f32[96,768]{1,0:T(8,128)S(1)} %get-tuple-element.5), channel_id=1, source_target_pairs={{0,2},{1,3},{2,4},{3,5},{4,6},{5,7},{6,0},{7,1},{8,10},{9,11},{10,... | collective-permute-start | bytes 884744 | tf_op jit(solution)/shard_map/ppermute | solution.py:33
  114.5 6.9 %collective-permute-start.9 = (f32[16,768]{1,0:T(8,128)S(1)}, f32[16,768]{1,0:T(8,128)S(1)}, u32[]{:S(2)}, u32[]{:S(2)}) collective-permute-start(f32[16,768]{1,0:T(8,128)S(1)} %add_add_fusion.3), channel_id=1, source_target_pairs={{0,65},{1,64},{2,67},{3,66},{4,69},{5,68},{6,71},{7,70},{64,1},{65... | collective-permute-start | bytes 147464 | tf_op jit(solution)/shard_map/ppermute | solution.py:51
  116.1 9.3 %collective-permute-start.8 = (f32[16,768]{1,0:T(8,128)S(1)}, f32[16,768]{1,0:T(8,128)S(1)}, u32[]{:S(2)}, u32[]{:S(2)}) collective-permute-start(f32[16,768]{1,0:T(8,128)S(1)} %add_add_fusion.3), channel_id=1, source_target_pairs={{0,64},{64,0},{1,65},{65,1},{2,66},{66,2},{3,67},{67,3},{4,68},{68... | collective-permute-start | bytes 147464 | tf_op jit(solution)/shard_map/ppermute | solution.py:49
  116.6 8.9 %collective-permute-start.7 = (f32[16,768]{1,0:T(8,128)S(1)}, f32[16,768]{1,0:T(8,128)S(1)}, u32[]{:S(2)}, u32[]{:S(2)}) collective-permute-start(f32[16,768]{1,0:T(8,128)S(1)} %add_add_fusion.3), channel_id=1, source_target_pairs={{0,1},{1,0},{2,3},{3,2},{4,5},{5,4},{6,7},{7,6},{8,9},{9,8},{10,11... | collective-permute-start | bytes 147464 | tf_op jit(solution)/shard_map/ppermute | solution.py:47
  120.7 8.4 %collective-permute-start.24 = (f32[24,768]{1,0:T(8,128)S(1)}, f32[24,768]{1,0:T(8,128)S(1)}, u32[]{:S(2)}, u32[]{:S(2)}) collective-permute-start(f32[24,768]{1,0:T(8,128)S(1)} %get-tuple-element.12), channel_id=1, source_target_pairs={{0,65},{1,64},{2,67},{3,66},{4,69},{5,68},{6,71},{7,70},{64,1},{65... | collective-permute-start | bytes 221192 | tf_op jit(solution)/shard_map/ppermute | solution.py:51
  121.1 8.0 %collective-permute-start.23 = (f32[24,768]{1,0:T(8,128)S(1)}, f32[24,768]{1,0:T(8,128)S(1)}, u32[]{:S(2)}, u32[]{:S(2)}) collective-permute-start(f32[24,768]{1,0:T(8,128)S(1)} %get-tuple-element.13), channel_id=1, source_target_pairs={{0,64},{64,0},{1,65},{65,1},{2,66},{66,2},{3,67},{67,3},{4,68},{68... | collective-permute-start | bytes 221192 | tf_op jit(solution)/shard_map/ppermute | solution.py:49
  121.4 7.7 %collective-permute-start.22 = (f32[24,768]{1,0:T(8,128)S(1)}, f32[24,768]{1,0:T(8,128)S(1)}, u32[]{:S(2)}, u32[]{:S(2)}) collective-permute-start(f32[24,768]{1,0:T(8,128)S(1)} %get-tuple-element.11), channel_id=1, source_target_pairs={{0,1},{1,0},{2,3},{3,2},{4,5},{5,4},{6,7},{7,6},{8,9},{9,8},{10,11... | collective-permute-start | bytes 221192 | tf_op jit(solution)/shard_map/ppermute | solution.py:47
  126.1 11.7 %collective-permute-start.10 = (f32[64,768]{1,0:T(8,128)S(1)}, f32[64,768]{1,0:T(8,128)S(1)}, u32[]{:S(2)}, u32[]{:S(2)}) collective-permute-start(f32[64,768]{1,0:T(8,128)S(1)} %bitcast_select_fusion.2), channel_id=1, source_target_pairs={{0,6},{1,7},{2,0},{3,1},{4,2},{5,3},{6,4},{7,5},{8,14},{9,15},{10,... | collective-permute-start | bytes 589832 | tf_op jit(solution)/shard_map/ppermute | solution.py:33
  128.9 9.0 %collective-permute-start.11 = (f32[64,768]{1,0:T(8,128)S(1)}, f32[64,768]{1,0:T(8,128)S(1)}, u32[]{:S(2)}, u32[]{:S(2)}) collective-permute-start(f32[64,768]{1,0:T(8,128)S(1)} %bitcast_select_fusion.2), channel_id=1, source_target_pairs={{0,4},{1,5},{2,6},{3,7},{4,0},{5,1},{6,2},{7,3},{8,12},{9,13},{10,... | collective-permute-start | bytes 589832 | tf_op jit(solution)/shard_map/ppermute | solution.py:33
  129.1 6.1 %collective-permute-start.27 = (f32[24,768]{1,0:T(8,128)S(1)}, f32[24,768]{1,0:T(8,128)S(1)}, u32[]{:S(2)}, u32[]{:S(2)}) collective-permute-start(f32[24,768]{1,0:T(8,128)S(1)} %add_add_fusion.2), channel_id=1, source_target_pairs={{0,65},{1,64},{2,67},{3,66},{4,69},{5,68},{6,71},{7,70},{64,1},{65... | collective-permute-start | bytes 221192 | tf_op jit(solution)/shard_map/ppermute | solution.py:51
  130.1 7.0 %collective-permute-start.26 = (f32[24,768]{1,0:T(8,128)S(1)}, f32[24,768]{1,0:T(8,128)S(1)}, u32[]{:S(2)}, u32[]{:S(2)}) collective-permute-start(f32[24,768]{1,0:T(8,128)S(1)} %add_add_fusion.2), channel_id=1, source_target_pairs={{0,64},{64,0},{1,65},{65,1},{2,66},{66,2},{3,67},{67,3},{4,68},{68... | collective-permute-start | bytes 221192 | tf_op jit(solution)/shard_map/ppermute | solution.py:49
  154.3 7.6 %collective-permute-start.14 = (f32[4096]{0:T(1024)S(1)}, f32[4096]{0:T(1024)S(1)}, u32[]{:S(2)}, u32[]{:S(2)}) collective-permute-start(f32[4096]{0:T(1024)S(1)} %reduce_max.9), channel_id=1, source_target_pairs={{0,16},{8,24},{16,0},{24,8},{32,48},{40,56},{48,32},{56,40},{1,17}... | collective-permute-start | bytes 49160 | tf_op jit(solution)/shard_map/ppermute | solution.py:82
  155.2 6.6 %collective-permute-start.13 = (f32[4096]{0:T(1024)S(1)}, f32[4096]{0:T(1024)S(1)}, u32[]{:S(2)}, u32[]{:S(2)}) collective-permute-start(f32[4096]{0:T(1024)S(1)} %reduce_max.9), channel_id=1, source_target_pairs={{0,8},{8,0},{16,24},{24,16},{32,40},{40,32},{48,56},{56,48},{1,9},... | collective-permute-start | bytes 49160 | tf_op jit(solution)/shard_map/ppermute | solution.py:82
  156.2 11.0 %collective-permute-start.28 = (f32[96,768]{1,0:T(8,128)S(1)}, f32[96,768]{1,0:T(8,128)S(1)}, u32[]{:S(2)}, u32[]{:S(2)}) collective-permute-start(f32[96,768]{1,0:T(8,128)S(1)} %bitcast_select_fusion), channel_id=1, source_target_pairs={{0,6},{1,7},{2,0},{3,1},{4,2},{5,3},{6,4},{7,5},{8,14},{9,15},{10,... | collective-permute-start | bytes 884744 | tf_op jit(solution)/shard_map/ppermute | solution.py:33
  159.5 13.2 %collective-permute-start.29 = (f32[96,768]{1,0:T(8,128)S(1)}, f32[96,768]{1,0:T(8,128)S(1)}, u32[]{:S(2)}, u32[]{:S(2)}) collective-permute-start(f32[96,768]{1,0:T(8,128)S(1)} %bitcast_select_fusion), channel_id=1, source_target_pairs={{0,4},{1,5},{2,6},{3,7},{4,0},{5,1},{6,2},{7,3},{8,12},{9,13},{10,... | collective-permute-start | bytes 884744 | tf_op jit(solution)/shard_map/ppermute | solution.py:33
  159.5 14.1 %collective-permute-start.30 = (f32[96,768]{1,0:T(8,128)S(1)}, f32[96,768]{1,0:T(8,128)S(1)}, u32[]{:S(2)}, u32[]{:S(2)}) collective-permute-start(f32[96,768]{1,0:T(8,128)S(1)} %bitcast_select_fusion), channel_id=1, source_target_pairs={{0,2},{1,3},{2,4},{3,5},{4,6},{5,7},{6,0},{7,1},{8,10},{9,11},{10,... | collective-permute-start | bytes 884744 | tf_op jit(solution)/shard_map/ppermute | solution.py:33
  189.6 7.5 %collective-permute-start.17 = (f32[4096]{0:T(1024)S(1)}, f32[4096]{0:T(1024)S(1)}, u32[]{:S(2)}, u32[]{:S(2)}) collective-permute-start(f32[4096]{0:T(1024)S(1)} %maximum_maximum_fusion), channel_id=1, source_target_pairs={{0,64},{64,0},{1,65},{65,1},{2,66},{66,2},{3,67},{67,3},{4,68},{68... | collective-permute-start | bytes 49160 | tf_op jit(solution)/shard_map/ppermute | solution.py:137
  (17 other events, 87.2 us)
Sparse Core Ops, SparseCore 0:
  9.7 69.5 all-gather.1
where the time goes:
time: 209 us
  waiting for transfers between devices  93.4 us (45%)
  starting transfers between devices  55.4 us (27%)
  matrix products  21.1 us (10%)
  local copies, waits for them, and re-layouts  17.6 us (8%)
  between operations  14.5 us (7%)
  other arithmetic  6.73 us (3%)
    all_gather x1, waiting for transfers between devices, body(): half = lax.all_gather(slab_embed, 'xc', axis=0, tiled=True)  65.1 us
    dot_general x2, matrix products, similar(): lax.dot_general(left, right, (((1,), (1,)), ((), ())), precision=lax.Prec...  21.1 us
    ppermute x12, starting transfers between devices, y_shift(): return lax.ppermute(value, 'col', pairs)  20 us
    ppermute x5, starting transfers between devices, z_group_shift(): return lax.ppermute(value, 'col', [(c, c ^ 1) for c in range(N_Y * N_Z)])  14.6 us
    gather x2, local copies, waits for them, and re-layouts, lookup(): jnp.take(source, jnp.clip(position, 0, source.shape[0] - 1), axis=0)  13 us
    ppermute x12, waiting for transfers between devices, y_shift(): return lax.ppermute(value, 'col', pairs)  11.7 us
    ppermute x5, starting transfers between devices, z_group_shift(): lax.ppermute(value, ('zl', 'col'), [(i, i ^ N_Y * N_Z ^ 1) for i in range...  7.06 us
    ppermute x3, starting transfers between devices, group_sum_in_order(): lax.ppermute(z_sum, 'col', pairs)  5.3 us
  transfers between devices with their start and end apart: 38, of which 18 were waited for; matrix products, arithmetic and copies ran while one was open for 6% of the time, Pallas kernels for 0%

commit v1 on v0

--- a/solution.py
+++ b/solution.py
@@ -119,7 +119,8 @@
     n_xc = 8
     col_id = lax.axis_index("col")
     zl = lax.axis_index("zl")
-    half = lax.all_gather(slab_embed, "xc", axis=0, tiled=True)
+    sent = jnp.stack([slab_embed] * lax.axis_size("xc"))
+    half = jnp.concatenate(lax.all_to_all(sent, "xc", 0, 0), axis=0)
     first_row = (col_id * 2 + zl) * half.shape[0]
     zl_swap = [(0, 1), (1, 0)]
     both_sel = pair_join(sel_index, lax.ppermute(sel_index, "zl", zl_swap), zl == 0)

time: 209 us -> 276 us (1.32)
  waiting for transfers between devices: 93.4 us -> 161 us
  between operations: 14.5 us -> 1.11 us
  local copies, waits for them, and re-layouts: 17.6 us -> 24.6 us
  starting transfers between devices: 55.4 us -> 60.8 us
    all_to_all x0 -> x1, waiting for transfers between devices: none -> 133 us  [body(): half = jnp.concatenate(lax.all_to_all(sent, 'xc', 0, 0), axis=0)]
    all_gather x1 -> x0, waiting for transfers between devices: 65.1 us -> none  [body(): half = lax.all_gather(slab_embed, 'xc', axis=0, tiled=True)]
    another operation x0 -> x1, local copies, waits for them, and re-layouts: none -> 7.01 us  [body(): sent = jnp.stack([slab_embed] * lax.axis_size('xc'))]
    all_to_all x0 -> x1, starting transfers between devices: none -> 5.5 us  [body(): half = jnp.concatenate(lax.all_to_all(sent, 'xc', 0, 0), axis=0)]
  transfers between devices with their start and end apart: 38 -> 38, of which waited for: 18 -> 17; matrix products, arithmetic and copies ran while one was open for 6% -> 4% of each run, Pallas kernels for 0% -> 0%
where the time goes in v1:
time: 276 us
  waiting for transfers between devices  161 us (58%)
  starting transfers between devices  60.8 us (22%)
  local copies, waits for them, and re-layouts  24.6 us (9%)
  matrix products  21.1 us (8%)
  other arithmetic  6.74 us (2%)
    all_to_all x1, waiting for transfers between devices, body(): half = jnp.concatenate(lax.all_to_all(sent, 'xc', 0, 0), axis=0)  133 us
    dot_general x2, matrix products, similar(): lax.dot_general(left, right, (((1,), (1,)), ((), ())), precision=lax.Prec...  21.1 us
    ppermute x12, starting transfers between devices, y_shift(): return lax.ppermute(value, 'col', pairs)  20.2 us
    ppermute x5, starting transfers between devices, z_group_shift(): return lax.ppermute(value, 'col', [(c, c ^ 1) for c in range(N_Y * N_Z)])  14.5 us
    gather x2, local copies, waits for them, and re-layouts, lookup(): jnp.take(source, jnp.clip(position, 0, source.shape[0] - 1), axis=0)  13 us
    ppermute x12, waiting for transfers between devices, y_shift(): return lax.ppermute(value, 'col', pairs)  10.8 us
    ppermute x5, starting transfers between devices, z_group_shift(): lax.ppermute(value, ('zl', 'col'), [(i, i ^ N_Y * N_Z ^ 1) for i in range...  8.57 us
    another operation x1, local copies, waits for them, and re-layouts, body(): sent = jnp.stack([slab_embed] * lax.axis_size('xc'))  7.01 us
  transfers between devices with their start and end apart: 38, of which 17 were waited for; matrix products, arithmetic and copies ran while one was open for 4% of the time, Pallas kernels for 0%

profile of v1, /device:TPU:8, one launch (start us, length us, event | category | flops | bytes accessed | tf_op | source)
XLA Modules:
  0.0 275.7 jit_solution(2479520542983121587)
XLA Ops:
  0.6 7.0 %stack.91 = f32[8,512,768]{2,1,0:T(8,128)} broadcast(f32[512,768]{1,0:T(8,128)} %param.6), dimensions={1,2} | broadcast | bytes 14155776 | tf_op jit(solution)/shard_map/stack | solution.py:122
  7.6 5.5 %all-to-all-start = ((f32[8,512,768]{2,1,0:T(8,128)}), f32[8,512,768]{2,1,0:T(8,128)}, u32[]{:S(2)}, u32[]{:S(2)}) async-start(f32[8,512,768]{2,1,0:T(8,128)} %stack.91), calls=%async_computation | async-start | bytes 25165824 | tf_op jit(solution)/shard_map/all_to_all | solution.py:123
  19.5 133.2 %all-to-all-done = f32[8,512,768]{2,1,0:T(8,128)} async-done(((f32[8,512,768]{2,1,0:T(8,128)}), f32[8,512,768]{2,1,0:T(8,128)}, u32[]{:S(2)}, u32[]{:S(2)}) %all-to-all-start) | async-done | bytes 12582944 | tf_op jit(solution)/shard_map/all_to_all | solution.py:123
  152.7 6.0 %gather_fusion = f32[256,768]{1,0:T(8,128)S(1)} fusion(f32[4096,768]{1,0:T(8,128)} %bitcast, s32[1024]{0:T(1024)S(1)} %pad_clamp_fusion.4), kind=kCustom, calls=%fused_computation.2 | custom fusion | bytes 1573888 | tf_op jit(solution)/shard_map/jit(_take)/gather | solution.py:23
  160.1 2.7 collective-permute-start.2
  164.6 7.1 %gather_fusion.2 = f32[384,768]{1,0:T(8,128)S(1)} fusion(f32[4096,768]{1,0:T(8,128)} %bitcast, s32[1024]{0:T(1024)S(1)} %pad_clamp_fusion.2), kind=kCustom, calls=%fused_computation.4 | custom fusion | bytes 2360832 | tf_op jit(solution)/shard_map/jit(_take)/gather | solution.py:23
  173.7 4.1 %collective-permute-start.6 = (f32[16,768]{1,0:T(8,128)S(1)}, f32[16,768]{1,0:T(8,128)S(1)}, u32[]{:S(2)}, u32[]{:S(2)}) collective-permute-start(f32[16,768]{1,0:T(8,128)S(1)} %get-tuple-element.15), channel_id=1, source_target_pairs={{0,65},{1,64},{2,67},{3,66},{4,69},{5,68},{6,71},{7,70},{64,1},{65... | collective-permute-start | bytes 147464 | tf_op jit(solution)/shard_map/ppermute | solution.py:51
  177.9 2.7 collective-permute-start.21
  180.7 2.0 collective-permute-start.19
  184.6 2.3 collective-permute-done.5
  190.6 2.5 collective-permute-start.7
  195.1 4.2 %collective-permute-start.22 = (f32[24,768]{1,0:T(8,128)S(1)}, f32[24,768]{1,0:T(8,128)S(1)}, u32[]{:S(2)}, u32[]{:S(2)}) collective-permute-start(f32[24,768]{1,0:T(8,128)S(1)} %get-tuple-element.11), channel_id=1, source_target_pairs={{0,1},{1,0},{2,3},{3,2},{4,5},{5,4},{6,7},{7,6},{8,9},{9,8},{10,11... | collective-permute-start | bytes 221192 | tf_op jit(solution)/shard_map/ppermute | solution.py:47
  199.9 2.7 collective-permute-start.10
  205.2 2.5 collective-permute-start.25
  211.7 3.3 %collective-permute-done.12 = f32[64,768]{1,0:T(8,128)S(1)} collective-permute-done((f32[64,768]{1,0:T(8,128)S(1)}, f32[64,768]{1,0:T(8,128)S(1)}, u32[]{:S(2)}, u32[]{:S(2)}) %collective-permute-start.12) | collective-permute-done | bytes 196640 | tf_op jit(solution)/shard_map/ppermute | solution.py:33
  215.2 10.3 %fusion.13 = f32[256,4096]{1,0:T(8,128)} fusion(f32[256,768]{1,0:T(8,128)S(1)} %bitcast.62, f32[4096,768]{1,0:T(8,128)} %bitcast), kind=kOutput, calls=%fused_computation.86 | convolution fusion | flops 4831838208 | bytes 17563648 | tf_op jit(solution)/shard_map/dot_general | solution.py:11
  225.5 2.4 reduce_max.9
  229.9 3.3 %collective-permute-start.28 = (f32[96,768]{1,0:T(8,128)S(1)}, f32[96,768]{1,0:T(8,128)S(1)}, u32[]{:S(2)}, u32[]{:S(2)}) collective-permute-start(f32[96,768]{1,0:T(8,128)S(1)} %bitcast_select_fusion), channel_id=1, source_target_pairs={{0,6},{1,7},{2,0},{3,1},{4,2},{5,3},{6,4},{7,5},{8,14},{9,15},{10,... | collective-permute-start | bytes 884744 | tf_op jit(solution)/shard_map/ppermute | solution.py:33
  233.2 2.3 collective-permute-start.30
  236.6 4.3 %collective-permute-done.16 = f32[4096]{0:T(1024)S(1)} collective-permute-done((f32[4096]{0:T(1024)S(1)}, f32[4096]{0:T(1024)S(1)}, u32[]{:S(2)}, u32[]{:S(2)}) %collective-permute-start.16) | collective-permute-done | bytes 16416 | tf_op jit(solution)/shard_map/ppermute | solution.py:82
  240.9 5.5 %collective-permute-done.29 = f32[96,768]{1,0:T(8,128)S(1)} collective-permute-done((f32[96,768]{1,0:T(8,128)S(1)}, f32[96,768]{1,0:T(8,128)S(1)}, u32[]{:S(2)}, u32[]{:S(2)}) %collective-permute-start.29) | collective-permute-done | bytes 294944 | tf_op jit(solution)/shard_map/ppermute | solution.py:33
  247.6 10.8 %maximum_reduce_fusion = f32[384]{0:T(512)S(1)} fusion(f32[384,768]{1,0:T(8,128)S(1)} %bitcast.65, f32[4096,768]{1,0:T(8,128)} %bitcast, f32[4096]{0:T(1024)S(1)} %maximum_maximum_fusion), kind=kOutput, calls=%fused_computation.6 | convolution fusion | flops 7252475392 | bytes 13780480 | tf_op jit(solution)/shard_map/dot_general | solution.py:11
  259.6 3.7 %collective-permute-start.31 = (f32[384]{0:T(512)S(1)}, f32[384]{0:T(512)S(1)}, u32[]{:S(2)}, u32[]{:S(2)}) collective-permute-start(f32[384]{0:T(512)S(1)} %maximum_reduce_fusion), channel_id=1, source_target_pairs={{0,1},{1,0},{2,3},{3,2},{4,5},{5,4},{6,7},{7,6},{8,9},{9,8},{10,11... | collective-permute-start | bytes 4616 | tf_op jit(solution)/shard_map/ppermute | solution.py:47
  267.0 3.9 %collective-permute-start.35 = (f32[384]{0:T(512)S(1)}, f32[384]{0:T(512)S(1)}, u32[]{:S(2)}, u32[]{:S(2)}) collective-permute-start(f32[384]{0:T(512)S(1)} %select_reduce_fusion.1), channel_id=1, source_target_pairs={{0,4},{1,5},{2,6},{3,7},{4,0},{5,1},{6,2},{7,3},{8,12},{9,13},{10,... | collective-permute-start | bytes 4616 | tf_op jit(solution)/shard_map/ppermute | solution.py:95
  (134 shorter events, 40.4 us)
Async XLA Ops:
  7.6 145.1 %all-to-all-start = ((f32[8,512,768]{2,1,0:T(8,128)}), f32[8,512,768]{2,1,0:T(8,128)}, u32[]{:S(2)}, u32[]{:S(2)}) async-start(f32[8,512,768]{2,1,0:T(8,128)} %stack.91), calls=%async_computation | async-start | bytes 25165824 | tf_op jit(solution)/shard_map/all_to_all | solution.py:123
  159.7 12.9 %collective-permute-start.3 = (f32[64,768]{1,0:T(8,128)}, f32[64,768]{1,0:T(8,128)S(1)}, u32[]{:S(2)}, u32[]{:S(2)}) collective-permute-start(f32[64,768]{1,0:T(8,128)} %get-tuple-element.9), channel_id=1, source_target_pairs={{0,6},{1,7},{2,0},{3,1},{4,2},{5,3},{6,4},{7,5},{8,14},{9,15},{10,... | collective-permute-start | bytes 589832 | tf_op jit(solution)/shard_map/ppermute | solution.py:33
  160.1 12.5 %collective-permute-start.2 = (f32[64,768]{1,0:T(8,128)}, f32[64,768]{1,0:T(8,128)}, u32[]{:S(2)}, u32[]{:S(2)}) collective-permute-start(f32[64,768]{1,0:T(8,128)} %get-tuple-element.10), channel_id=1, source_target_pairs={{0,4},{1,5},{2,6},{3,7},{4,0},{5,1},{6,2},{7,3},{8,12},{9,13},{10,... | collective-permute-start | bytes 589832 | tf_op jit(solution)/shard_map/ppermute | solution.py:33
  162.7 9.8 %collective-permute-start.1 = (f32[64,768]{1,0:T(8,128)S(1)}, f32[64,768]{1,0:T(8,128)}, u32[]{:S(2)}, u32[]{:S(2)}) collective-permute-start(f32[64,768]{1,0:T(8,128)S(1)} %get-tuple-element.8), channel_id=1, source_target_pairs={{0,2},{1,3},{2,4},{3,5},{4,6},{5,7},{6,0},{7,1},{8,10},{9,11},{10,... | collective-permute-start | bytes 589832 | tf_op jit(solution)/shard_map/ppermute | solution.py:33
  173.7 9.1 %collective-permute-start.6 = (f32[16,768]{1,0:T(8,128)S(1)}, f32[16,768]{1,0:T(8,128)S(1)}, u32[]{:S(2)}, u32[]{:S(2)}) collective-permute-start(f32[16,768]{1,0:T(8,128)S(1)} %get-tuple-element.15), channel_id=1, source_target_pairs={{0,65},{1,64},{2,67},{3,66},{4,69},{5,68},{6,71},{7,70},{64,1},{65... | collective-permute-start | bytes 147464 | tf_op jit(solution)/shard_map/ppermute | solution.py:51
  177.9 12.8 %collective-permute-start.21 = (f32[96,768]{1,0:T(8,128)S(1)}, f32[96,768]{1,0:T(8,128)S(1)}, u32[]{:S(2)}, u32[]{:S(2)}) collective-permute-start(f32[96,768]{1,0:T(8,128)S(1)} %get-tuple-element.6), channel_id=1, source_target_pairs={{0,6},{1,7},{2,0},{3,1},{4,2},{5,3},{6,4},{7,5},{8,14},{9,15},{10,... | collective-permute-start | bytes 884744 | tf_op jit(solution)/shard_map/ppermute | solution.py:33
  180.6 13.1 %collective-permute-start.20 = (f32[96,768]{1,0:T(8,128)S(1)}, f32[96,768]{1,0:T(8,128)S(1)}, u32[]{:S(2)}, u32[]{:S(2)}) collective-permute-start(f32[96,768]{1,0:T(8,128)S(1)} %get-tuple-element.7), channel_id=1, source_target_pairs={{0,4},{1,5},{2,6},{3,7},{4,0},{5,1},{6,2},{7,3},{8,12},{9,13},{10,... | collective-permute-start | bytes 884744 | tf_op jit(solution)/shard_map/ppermute | solution.py:33
  180.7 13.6 %collective-permute-start.19 = (f32[96,768]{1,0:T(8,128)S(1)}, f32[96,768]{1,0:T(8,128)S(1)}, u32[]{:S(2)}, u32[]{:S(2)}) collective-permute-start(f32[96,768]{1,0:T(8,128)S(1)} %get-tuple-element.5), channel_id=1, source_target_pairs={{0,2},{1,3},{2,4},{3,5},{4,6},{5,7},{6,0},{7,1},{8,10},{9,11},{10,... | collective-permute-start | bytes 884744 | tf_op jit(solution)/shard_map/ppermute | solution.py:33
  188.4 6.7 %collective-permute-start.9 = (f32[16,768]{1,0:T(8,128)S(1)}, f32[16,768]{1,0:T(8,128)S(1)}, u32[]{:S(2)}, u32[]{:S(2)}) collective-permute-start(f32[16,768]{1,0:T(8,128)S(1)} %add_add_fusion.3), channel_id=1, source_target_pairs={{0,65},{1,64},{2,67},{3,66},{4,69},{5,68},{6,71},{7,70},{64,1},{65... | collective-permute-start | bytes 147464 | tf_op jit(solution)/shard_map/ppermute | solution.py:51
  190.2 9.1 %collective-permute-start.8 = (f32[16,768]{1,0:T(8,128)S(1)}, f32[16,768]{1,0:T(8,128)S(1)}, u32[]{:S(2)}, u32[]{:S(2)}) collective-permute-start(f32[16,768]{1,0:T(8,128)S(1)} %add_add_fusion.3), channel_id=1, source_target_pairs={{0,64},{64,0},{1,65},{65,1},{2,66},{66,2},{3,67},{67,3},{4,68},{68... | collective-permute-start | bytes 147464 | tf_op jit(solution)/shard_map/ppermute | solution.py:49
  190.6 8.6 %collective-permute-start.7 = (f32[16,768]{1,0:T(8,128)S(1)}, f32[16,768]{1,0:T(8,128)S(1)}, u32[]{:S(2)}, u32[]{:S(2)}) collective-permute-start(f32[16,768]{1,0:T(8,128)S(1)} %add_add_fusion.3), channel_id=1, source_target_pairs={{0,1},{1,0},{2,3},{3,2},{4,5},{5,4},{6,7},{7,6},{8,9},{9,8},{10,11... | collective-permute-start | bytes 147464 | tf_op jit(solution)/shard_map/ppermute | solution.py:47
  194.5 8.4 %collective-permute-start.24 = (f32[24,768]{1,0:T(8,128)S(1)}, f32[24,768]{1,0:T(8,128)S(1)}, u32[]{:S(2)}, u32[]{:S(2)}) collective-permute-start(f32[24,768]{1,0:T(8,128)S(1)} %get-tuple-element.12), channel_id=1, source_target_pairs={{0,65},{1,64},{2,67},{3,66},{4,69},{5,68},{6,71},{7,70},{64,1},{65... | collective-permute-start | bytes 221192 | tf_op jit(solution)/shard_map/ppermute | solution.py:51
  195.1 7.8 %collective-permute-start.23 = (f32[24,768]{1,0:T(8,128)S(1)}, f32[24,768]{1,0:T(8,128)S(1)}, u32[]{:S(2)}, u32[]{:S(2)}) collective-permute-start(f32[24,768]{1,0:T(8,128)S(1)} %get-tuple-element.13), channel_id=1, source_target_pairs={{0,64},{64,0},{1,65},{65,1},{2,66},{66,2},{3,67},{67,3},{4,68},{68... | collective-permute-start | bytes 221192 | tf_op jit(solution)/shard_map/ppermute | solution.py:49
  195.1 7.8 %collective-permute-start.22 = (f32[24,768]{1,0:T(8,128)S(1)}, f32[24,768]{1,0:T(8,128)S(1)}, u32[]{:S(2)}, u32[]{:S(2)}) collective-permute-start(f32[24,768]{1,0:T(8,128)S(1)} %get-tuple-element.11), channel_id=1, source_target_pairs={{0,1},{1,0},{2,3},{3,2},{4,5},{5,4},{6,7},{7,6},{8,9},{9,8},{10,11... | collective-permute-start | bytes 221192 | tf_op jit(solution)/shard_map/ppermute | solution.py:47
  199.9 11.7 %collective-permute-start.10 = (f32[64,768]{1,0:T(8,128)S(1)}, f32[64,768]{1,0:T(8,128)S(1)}, u32[]{:S(2)}, u32[]{:S(2)}) collective-permute-start(f32[64,768]{1,0:T(8,128)S(1)} %bitcast_select_fusion.2), channel_id=1, source_target_pairs={{0,6},{1,7},{2,0},{3,1},{4,2},{5,3},{6,4},{7,5},{8,14},{9,15},{10,... | collective-permute-start | bytes 589832 | tf_op jit(solution)/shard_map/ppermute | solution.py:33
  202.6 9.1 %collective-permute-start.11 = (f32[64,768]{1,0:T(8,128)S(1)}, f32[64,768]{1,0:T(8,128)S(1)}, u32[]{:S(2)}, u32[]{:S(2)}) collective-permute-start(f32[64,768]{1,0:T(8,128)S(1)} %bitcast_select_fusion.2), channel_id=1, source_target_pairs={{0,4},{1,5},{2,6},{3,7},{4,0},{5,1},{6,2},{7,3},{8,12},{9,13},{10,... | collective-permute-start | bytes 589832 | tf_op jit(solution)/shard_map/ppermute | solution.py:33
  202.9 6.1 %collective-permute-start.27 = (f32[24,768]{1,0:T(8,128)S(1)}, f32[24,768]{1,0:T(8,128)S(1)}, u32[]{:S(2)}, u32[]{:S(2)}) collective-permute-start(f32[24,768]{1,0:T(8,128)S(1)} %add_add_fusion.2), channel_id=1, source_target_pairs={{0,65},{1,64},{2,67},{3,66},{4,69},{5,68},{6,71},{7,70},{64,1},{65... | collective-permute-start | bytes 221192 | tf_op jit(solution)/shard_map/ppermute | solution.py:51
  204.0 6.9 %collective-permute-start.26 = (f32[24,768]{1,0:T(8,128)S(1)}, f32[24,768]{1,0:T(8,128)S(1)}, u32[]{:S(2)}, u32[]{:S(2)}) collective-permute-start(f32[24,768]{1,0:T(8,128)S(1)} %add_add_fusion.2), channel_id=1, source_target_pairs={{0,64},{64,0},{1,65},{65,1},{2,66},{66,2},{3,67},{67,3},{4,68},{68... | collective-permute-start | bytes 221192 | tf_op jit(solution)/shard_map/ppermute | solution.py:49
  228.0 7.6 %collective-permute-start.14 = (f32[4096]{0:T(1024)S(1)}, f32[4096]{0:T(1024)S(1)}, u32[]{:S(2)}, u32[]{:S(2)}) collective-permute-start(f32[4096]{0:T(1024)S(1)} %reduce_max.9), channel_id=1, source_target_pairs={{0,16},{8,24},{16,0},{24,8},{32,48},{40,56},{48,32},{56,40},{1,17}... | collective-permute-start | bytes 49160 | tf_op jit(solution)/shard_map/ppermute | solution.py:82
  228.6 6.9 %collective-permute-start.13 = (f32[4096]{0:T(1024)S(1)}, f32[4096]{0:T(1024)S(1)}, u32[]{:S(2)}, u32[]{:S(2)}) collective-permute-start(f32[4096]{0:T(1024)S(1)} %reduce_max.9), channel_id=1, source_target_pairs={{0,8},{8,0},{16,24},{24,16},{32,40},{40,32},{48,56},{56,48},{1,9},... | collective-permute-start | bytes 49160 | tf_op jit(solution)/shard_map/ppermute | solution.py:82
  229.9 11.0 %collective-permute-start.28 = (f32[96,768]{1,0:T(8,128)S(1)}, f32[96,768]{1,0:T(8,128)S(1)}, u32[]{:S(2)}, u32[]{:S(2)}) collective-permute-start(f32[96,768]{1,0:T(8,128)S(1)} %bitcast_select_fusion), channel_id=1, source_target_pairs={{0,6},{1,7},{2,0},{3,1},{4,2},{5,3},{6,4},{7,5},{8,14},{9,15},{10,... | collective-permute-start | bytes 884744 | tf_op jit(solution)/shard_map/ppermute | solution.py:33
  233.2 13.2 %collective-permute-start.29 = (f32[96,768]{1,0:T(8,128)S(1)}, f32[96,768]{1,0:T(8,128)S(1)}, u32[]{:S(2)}, u32[]{:S(2)}) collective-permute-start(f32[96,768]{1,0:T(8,128)S(1)} %bitcast_select_fusion), channel_id=1, source_target_pairs={{0,4},{1,5},{2,6},{3,7},{4,0},{5,1},{6,2},{7,3},{8,12},{9,13},{10,... | collective-permute-start | bytes 884744 | tf_op jit(solution)/shard_map/ppermute | solution.py:33
  233.2 14.1 %collective-permute-start.30 = (f32[96,768]{1,0:T(8,128)S(1)}, f32[96,768]{1,0:T(8,128)S(1)}, u32[]{:S(2)}, u32[]{:S(2)}) collective-permute-start(f32[96,768]{1,0:T(8,128)S(1)} %bitcast_select_fusion), channel_id=1, source_target_pairs={{0,2},{1,3},{2,4},{3,5},{4,6},{5,7},{6,0},{7,1},{8,10},{9,11},{10,... | collective-permute-start | bytes 884744 | tf_op jit(solution)/shard_map/ppermute | solution.py:33
  263.3 7.6 %collective-permute-start.17 = (f32[4096]{0:T(1024)S(1)}, f32[4096]{0:T(1024)S(1)}, u32[]{:S(2)}, u32[]{:S(2)}) collective-permute-start(f32[4096]{0:T(1024)S(1)} %maximum_maximum_fusion), channel_id=1, source_target_pairs={{0,64},{64,0},{1,65},{65,1},{2,66},{66,2},{3,67},{67,3},{4,68},{68... | collective-permute-start | bytes 49160 | tf_op jit(solution)/shard_map/ppermute | solution.py:138
  (17 other events, 96.7 us)
